TPU v7x, 512 devices: a whole 4x8x8 slice. The times are simulated.
512 devices in a mesh: sep: 8 (over y), row: 8 (over z), col: 8 (over x, core).
Axes of the slice: x: 4, y: 8, z: 8, core: 2. Of those that a mesh axis runs over, the one named last changes fastest.
Arguments:
- right_sides: float32 [2, 16, 32768], P(None, None, ('sep', 'row', 'col')), may hold values from -6 to 6
- inverse_diag: float32 [8, 4096, 4096], P('sep', ('row', 'col')), may hold values from -0.09375 to 0.09375
- lower_blocks: float32 [8, 2048, 4096], P('sep', ('row', 'col')), may hold values from -0.09375 to 0.09375
- targets: int32 [8, 2048], P('sep', ('row', 'col')), may hold values from 0 to 32767, as said below
- counts: int32 [8, 64], P('sep', ('row', 'col')), may hold values from 0 to 32, as said below
Outputs:
- solution: float32 [2, 16, 32768], P(None, None, ('sep', 'row', 'col'))
Inputs may be any that keep to these rules, and one draw needn't show every extreme that they name: For every separator s and lower row j: targets[s, j] // 4096 > s, except for the last separator whose counts are all zero; and (targets[s, j] % 4096) // 64 == j // 32. The last separator's counts are zero; every other separator has a block with exactly 32 live rows, and the others at least one.
All inputs are finite; a program needn't handle non-finite values.
Results may differ from a plain program's by a relative error of at most 0.0001.
Values sent between devices are 32-bit elements; how exact they have to be, the bound alone decides.
No kernel may reach another device: no remote copies, remote signals or barrier semaphores. Data moves between devices by JAX's collectives and lax.ppermute only.
A program may use at most 64 MiB of HBM per device.

v0:
```python
import jax
import jax.numpy as jnp
from jax import lax
from jax.sharding import PartitionSpec as P

W = 4096


def passed_along(block, axis, distance):
    devices = range(lax.axis_size(axis))
    route = [(i - distance, i) for i in devices if i - distance in devices]
    return lax.ppermute(block, axis, route)


def shards(right_sides, inverse_diag, lower_blocks, targets, counts):
    levels = lax.axis_size("sep")
    own_level = lax.axis_index("sep")
    batches = right_sides.shape[0]
    width_rhs = right_sides.shape[1]
    own_rows = right_sides.shape[2]
    diag_rows = inverse_diag[0]
    lower_rows = lower_blocks[0]
    lower_count = lower_rows.shape[0]
    live = jnp.arange(lower_count, dtype=jnp.int32) < counts[0, 0]
    places = targets[0] // W * own_rows + targets[0] % own_rows

    def solve_piece(segment):
        return lax.dot_general(
            segment,
            diag_rows,
            (((1,), (1,)), ((), ())),
            precision=lax.Precision.HIGHEST,
            preferred_element_type=jnp.float32,
        )

    def lower_piece(segment):
        return lax.dot_general(
            segment,
            lower_rows,
            (((1,), (1,)), ((), ())),
            precision=lax.Precision.HIGHEST,
            preferred_element_type=jnp.float32,
        )

    def one_turn(turn, state):
        carried, solved_all = state
        batch_now = turn // levels
        active = turn % levels == own_level
        batch_now = jnp.clip(batch_now, 0, batches - 1)
        given = lax.dynamic_index_in_dim(right_sides, batch_now, 0, keepdims=False)
        resid = given - lax.dynamic_slice_in_dim(carried, own_level * own_rows, own_rows, 1)
        solved = solve_piece(lax.all_gather(resid, ("row", "col"), axis=1, tiled=True))
        update = lower_piece(lax.all_gather(solved, ("row", "col"), axis=1, tiled=True))
        update = jnp.where(live[None, :], update, jnp.float32(0.0))
        carried = carried.at[:, places].add(update)
        former = lax.dynamic_index_in_dim(solved_all, batch_now, 0, keepdims=False)
        solved_all = lax.dynamic_update_index_in_dim(
            solved_all, jnp.where(active, solved, former), batch_now, 0
        )
        carried = passed_along(carried, "sep", 1)
        return (carried, solved_all)

    turns = batches * levels
    start_carry = jnp.zeros((width_rhs, levels * own_rows), jnp.float32)
    start_solved = jnp.zeros(right_sides.shape, jnp.float32)
    final_carry, solution = lax.fori_loop(0, turns, one_turn, (start_carry, start_solved))
    return solution


def solution(mesh):
    placed = (
        P(None, None, ("sep", "row", "col")),
        P("sep", ("row", "col"), None),
        P("sep", ("row", "col"), None),
        P("sep", ("row", "col")),
        P("sep", ("row", "col")),
    )
    return jax.shard_map(
        shards,
        mesh=mesh,
        in_specs=placed,
        out_specs=P(None, None, ("sep", "row", "col")),
        check_vma=False,
    )
```

profile of v0, /device:TPU:32, one launch (start us, length us, event | category | flops | bytes accessed | tf_op | source)
XLA Modules:
  0.0 1837.8 jit_solution(4809233854240847362)
XLA Ops:
  1.4 1835.8 %while.18 = (s32[]{:T(128)}, f32[16,512]{0,1:T(8,128)S(1)}, f32[2,16,64]{2,1,0:T(8,128)S(1)}, s32[32]{0:T(128)S(1)}, f32[2,16,64]{2,1,0:T(8,128)S(1)}, /*index=5...) while((s32[]{:T(128)}, f32[16,512]{0,1:T(8,128)S(1)}, ...), condition=%wide.region_2.3_spmd.clone, body=%wide.region_0.2_spmd.clone.sunk | while | flops 75500688 | bytes 11338590 | solution.py:66
  1.6 56.5 %all-gather.6 = f32[64,64,16]{1,2,0:T(8,128)S(1)} all-gather(f32[1,64,16]{1,2,0:T(8,128)S(1)} %fusion.22), channel_id=1, replica_groups=mesh['sep'=8,'row'=8,'col'=8] {'row','col'}, dimensions={0}, use_global_device_ids=true | all-gather | bytes 266240 | tf_op jit(solution)/shard_map/while/body/eval_jaxpr/all_gather | solution.py:52
  60.2 49.5 %all-gather.7 = f32[64,64,16]{1,2,0:T(8,128)S(1)} all-gather(f32[1,64,16]{1,2,0:T(8,128)S(1)} %bitcast.71), channel_id=1, replica_groups=mesh['sep'=8,'row'=8,'col'=8] {'row','col'}, dimensions={0}, use_global_device_ids=true | all-gather | bytes 266240 | tf_op jit(solution)/shard_map/while/body/eval_jaxpr/all_gather | solution.py:53
  124.3 48.0 %all-gather.6 = f32[64,64,16]{1,2,0:T(8,128)S(1)} all-gather(f32[1,64,16]{1,2,0:T(8,128)S(1)} %fusion.22), channel_id=1, replica_groups=mesh['sep'=8,'row'=8,'col'=8] {'row','col'}, dimensions={0}, use_global_device_ids=true | all-gather | bytes 266240 | tf_op jit(solution)/shard_map/while/body/eval_jaxpr/all_gather | solution.py:52
  174.4 49.5 %all-gather.7 = f32[64,64,16]{1,2,0:T(8,128)S(1)} all-gather(f32[1,64,16]{1,2,0:T(8,128)S(1)} %bitcast.71), channel_id=1, replica_groups=mesh['sep'=8,'row'=8,'col'=8] {'row','col'}, dimensions={0}, use_global_device_ids=true | all-gather | bytes 266240 | tf_op jit(solution)/shard_map/while/body/eval_jaxpr/all_gather | solution.py:53
  228.6 9.7 collective-permute-done
  238.5 48.0 %all-gather.6 = f32[64,64,16]{1,2,0:T(8,128)S(1)} all-gather(f32[1,64,16]{1,2,0:T(8,128)S(1)} %fusion.22), channel_id=1, replica_groups=mesh['sep'=8,'row'=8,'col'=8] {'row','col'}, dimensions={0}, use_global_device_ids=true | all-gather | bytes 266240 | tf_op jit(solution)/shard_map/while/body/eval_jaxpr/all_gather | solution.py:52
  288.6 49.5 %all-gather.7 = f32[64,64,16]{1,2,0:T(8,128)S(1)} all-gather(f32[1,64,16]{1,2,0:T(8,128)S(1)} %bitcast.71), channel_id=1, replica_groups=mesh['sep'=8,'row'=8,'col'=8] {'row','col'}, dimensions={0}, use_global_device_ids=true | all-gather | bytes 266240 | tf_op jit(solution)/shard_map/while/body/eval_jaxpr/all_gather | solution.py:53
  342.8 9.7 collective-permute-done
  352.7 48.0 %all-gather.6 = f32[64,64,16]{1,2,0:T(8,128)S(1)} all-gather(f32[1,64,16]{1,2,0:T(8,128)S(1)} %fusion.22), channel_id=1, replica_groups=mesh['sep'=8,'row'=8,'col'=8] {'row','col'}, dimensions={0}, use_global_device_ids=true | all-gather | bytes 266240 | tf_op jit(solution)/shard_map/while/body/eval_jaxpr/all_gather | solution.py:52
  402.8 49.5 %all-gather.7 = f32[64,64,16]{1,2,0:T(8,128)S(1)} all-gather(f32[1,64,16]{1,2,0:T(8,128)S(1)} %bitcast.71), channel_id=1, replica_groups=mesh['sep'=8,'row'=8,'col'=8] {'row','col'}, dimensions={0}, use_global_device_ids=true | all-gather | bytes 266240 | tf_op jit(solution)/shard_map/while/body/eval_jaxpr/all_gather | solution.py:53
  457.0 9.7 collective-permute-done
  467.0 48.0 %all-gather.6 = f32[64,64,16]{1,2,0:T(8,128)S(1)} all-gather(f32[1,64,16]{1,2,0:T(8,128)S(1)} %fusion.22), channel_id=1, replica_groups=mesh['sep'=8,'row'=8,'col'=8] {'row','col'}, dimensions={0}, use_global_device_ids=true | all-gather | bytes 266240 | tf_op jit(solution)/shard_map/while/body/eval_jaxpr/all_gather | solution.py:52
  517.0 49.5 %all-gather.7 = f32[64,64,16]{1,2,0:T(8,128)S(1)} all-gather(f32[1,64,16]{1,2,0:T(8,128)S(1)} %bitcast.71), channel_id=1, replica_groups=mesh['sep'=8,'row'=8,'col'=8] {'row','col'}, dimensions={0}, use_global_device_ids=true | all-gather | bytes 266240 | tf_op jit(solution)/shard_map/while/body/eval_jaxpr/all_gather | solution.py:53
  571.2 9.7 collective-permute-done
  581.2 48.0 %all-gather.6 = f32[64,64,16]{1,2,0:T(8,128)S(1)} all-gather(f32[1,64,16]{1,2,0:T(8,128)S(1)} %fusion.22), channel_id=1, replica_groups=mesh['sep'=8,'row'=8,'col'=8] {'row','col'}, dimensions={0}, use_global_device_ids=true | all-gather | bytes 266240 | tf_op jit(solution)/shard_map/while/body/eval_jaxpr/all_gather | solution.py:52
  631.3 49.5 %all-gather.7 = f32[64,64,16]{1,2,0:T(8,128)S(1)} all-gather(f32[1,64,16]{1,2,0:T(8,128)S(1)} %bitcast.71), channel_id=1, replica_groups=mesh['sep'=8,'row'=8,'col'=8] {'row','col'}, dimensions={0}, use_global_device_ids=true | all-gather | bytes 266240 | tf_op jit(solution)/shard_map/while/body/eval_jaxpr/all_gather | solution.py:53
  685.4 9.7 collective-permute-done
  695.4 48.0 %all-gather.6 = f32[64,64,16]{1,2,0:T(8,128)S(1)} all-gather(f32[1,64,16]{1,2,0:T(8,128)S(1)} %fusion.22), channel_id=1, replica_groups=mesh['sep'=8,'row'=8,'col'=8] {'row','col'}, dimensions={0}, use_global_device_ids=true | all-gather | bytes 266240 | tf_op jit(solution)/shard_map/while/body/eval_jaxpr/all_gather | solution.py:52
  745.5 49.5 %all-gather.7 = f32[64,64,16]{1,2,0:T(8,128)S(1)} all-gather(f32[1,64,16]{1,2,0:T(8,128)S(1)} %bitcast.71), channel_id=1, replica_groups=mesh['sep'=8,'row'=8,'col'=8] {'row','col'}, dimensions={0}, use_global_device_ids=true | all-gather | bytes 266240 | tf_op jit(solution)/shard_map/while/body/eval_jaxpr/all_gather | solution.py:53
  799.6 9.7 collective-permute-done
  809.6 48.0 %all-gather.6 = f32[64,64,16]{1,2,0:T(8,128)S(1)} all-gather(f32[1,64,16]{1,2,0:T(8,128)S(1)} %fusion.22), channel_id=1, replica_groups=mesh['sep'=8,'row'=8,'col'=8] {'row','col'}, dimensions={0}, use_global_device_ids=true | all-gather | bytes 266240 | tf_op jit(solution)/shard_map/while/body/eval_jaxpr/all_gather | solution.py:52
  859.7 49.5 %all-gather.7 = f32[64,64,16]{1,2,0:T(8,128)S(1)} all-gather(f32[1,64,16]{1,2,0:T(8,128)S(1)} %bitcast.71), channel_id=1, replica_groups=mesh['sep'=8,'row'=8,'col'=8] {'row','col'}, dimensions={0}, use_global_device_ids=true | all-gather | bytes 266240 | tf_op jit(solution)/shard_map/while/body/eval_jaxpr/all_gather | solution.py:53
  913.8 9.7 collective-permute-done
  923.8 48.0 %all-gather.6 = f32[64,64,16]{1,2,0:T(8,128)S(1)} all-gather(f32[1,64,16]{1,2,0:T(8,128)S(1)} %fusion.22), channel_id=1, replica_groups=mesh['sep'=8,'row'=8,'col'=8] {'row','col'}, dimensions={0}, use_global_device_ids=true | all-gather | bytes 266240 | tf_op jit(solution)/shard_map/while/body/eval_jaxpr/all_gather | solution.py:52
  973.9 49.5 %all-gather.7 = f32[64,64,16]{1,2,0:T(8,128)S(1)} all-gather(f32[1,64,16]{1,2,0:T(8,128)S(1)} %bitcast.71), channel_id=1, replica_groups=mesh['sep'=8,'row'=8,'col'=8] {'row','col'}, dimensions={0}, use_global_device_ids=true | all-gather | bytes 266240 | tf_op jit(solution)/shard_map/while/body/eval_jaxpr/all_gather | solution.py:53
  1028.0 9.7 collective-permute-done
  1038.0 48.0 %all-gather.6 = f32[64,64,16]{1,2,0:T(8,128)S(1)} all-gather(f32[1,64,16]{1,2,0:T(8,128)S(1)} %fusion.22), channel_id=1, replica_groups=mesh['sep'=8,'row'=8,'col'=8] {'row','col'}, dimensions={0}, use_global_device_ids=true | all-gather | bytes 266240 | tf_op jit(solution)/shard_map/while/body/eval_jaxpr/all_gather | solution.py:52
  1088.1 49.5 %all-gather.7 = f32[64,64,16]{1,2,0:T(8,128)S(1)} all-gather(f32[1,64,16]{1,2,0:T(8,128)S(1)} %bitcast.71), channel_id=1, replica_groups=mesh['sep'=8,'row'=8,'col'=8] {'row','col'}, dimensions={0}, use_global_device_ids=true | all-gather | bytes 266240 | tf_op jit(solution)/shard_map/while/body/eval_jaxpr/all_gather | solution.py:53
  1142.2 9.7 collective-permute-done
  1152.2 48.0 %all-gather.6 = f32[64,64,16]{1,2,0:T(8,128)S(1)} all-gather(f32[1,64,16]{1,2,0:T(8,128)S(1)} %fusion.22), channel_id=1, replica_groups=mesh['sep'=8,'row'=8,'col'=8] {'row','col'}, dimensions={0}, use_global_device_ids=true | all-gather | bytes 266240 | tf_op jit(solution)/shard_map/while/body/eval_jaxpr/all_gather | solution.py:52
  1202.3 49.5 %all-gather.7 = f32[64,64,16]{1,2,0:T(8,128)S(1)} all-gather(f32[1,64,16]{1,2,0:T(8,128)S(1)} %bitcast.71), channel_id=1, replica_groups=mesh['sep'=8,'row'=8,'col'=8] {'row','col'}, dimensions={0}, use_global_device_ids=true | all-gather | bytes 266240 | tf_op jit(solution)/shard_map/while/body/eval_jaxpr/all_gather | solution.py:53
  1256.4 9.7 collective-permute-done
  1266.4 48.0 %all-gather.6 = f32[64,64,16]{1,2,0:T(8,128)S(1)} all-gather(f32[1,64,16]{1,2,0:T(8,128)S(1)} %fusion.22), channel_id=1, replica_groups=mesh['sep'=8,'row'=8,'col'=8] {'row','col'}, dimensions={0}, use_global_device_ids=true | all-gather | bytes 266240 | tf_op jit(solution)/shard_map/while/body/eval_jaxpr/all_gather | solution.py:52
  1316.5 49.5 %all-gather.7 = f32[64,64,16]{1,2,0:T(8,128)S(1)} all-gather(f32[1,64,16]{1,2,0:T(8,128)S(1)} %bitcast.71), channel_id=1, replica_groups=mesh['sep'=8,'row'=8,'col'=8] {'row','col'}, dimensions={0}, use_global_device_ids=true | all-gather | bytes 266240 | tf_op jit(solution)/shard_map/while/body/eval_jaxpr/all_gather | solution.py:53
  1370.6 9.7 collective-permute-done
  1380.6 48.0 %all-gather.6 = f32[64,64,16]{1,2,0:T(8,128)S(1)} all-gather(f32[1,64,16]{1,2,0:T(8,128)S(1)} %fusion.22), channel_id=1, replica_groups=mesh['sep'=8,'row'=8,'col'=8] {'row','col'}, dimensions={0}, use_global_device_ids=true | all-gather | bytes 266240 | tf_op jit(solution)/shard_map/while/body/eval_jaxpr/all_gather | solution.py:52
  1430.7 49.5 %all-gather.7 = f32[64,64,16]{1,2,0:T(8,128)S(1)} all-gather(f32[1,64,16]{1,2,0:T(8,128)S(1)} %bitcast.71), channel_id=1, replica_groups=mesh['sep'=8,'row'=8,'col'=8] {'row','col'}, dimensions={0}, use_global_device_ids=true | all-gather | bytes 266240 | tf_op jit(solution)/shard_map/while/body/eval_jaxpr/all_gather | solution.py:53
  1484.8 9.7 collective-permute-done
  1494.8 48.0 %all-gather.6 = f32[64,64,16]{1,2,0:T(8,128)S(1)} all-gather(f32[1,64,16]{1,2,0:T(8,128)S(1)} %fusion.22), channel_id=1, replica_groups=mesh['sep'=8,'row'=8,'col'=8] {'row','col'}, dimensions={0}, use_global_device_ids=true | all-gather | bytes 266240 | tf_op jit(solution)/shard_map/while/body/eval_jaxpr/all_gather | solution.py:52
  1544.9 49.5 %all-gather.7 = f32[64,64,16]{1,2,0:T(8,128)S(1)} all-gather(f32[1,64,16]{1,2,0:T(8,128)S(1)} %bitcast.71), channel_id=1, replica_groups=mesh['sep'=8,'row'=8,'col'=8] {'row','col'}, dimensions={0}, use_global_device_ids=true | all-gather | bytes 266240 | tf_op jit(solution)/shard_map/while/body/eval_jaxpr/all_gather | solution.py:53
  1599.0 9.7 collective-permute-done
  1609.0 48.0 %all-gather.6 = f32[64,64,16]{1,2,0:T(8,128)S(1)} all-gather(f32[1,64,16]{1,2,0:T(8,128)S(1)} %fusion.22), channel_id=1, replica_groups=mesh['sep'=8,'row'=8,'col'=8] {'row','col'}, dimensions={0}, use_global_device_ids=true | all-gather | bytes 266240 | tf_op jit(solution)/shard_map/while/body/eval_jaxpr/all_gather | solution.py:52
  1659.1 49.5 %all-gather.7 = f32[64,64,16]{1,2,0:T(8,128)S(1)} all-gather(f32[1,64,16]{1,2,0:T(8,128)S(1)} %bitcast.71), channel_id=1, replica_groups=mesh['sep'=8,'row'=8,'col'=8] {'row','col'}, dimensions={0}, use_global_device_ids=true | all-gather | bytes 266240 | tf_op jit(solution)/shard_map/while/body/eval_jaxpr/all_gather | solution.py:53
  1713.2 9.7 collective-permute-done
  1723.2 48.0 %all-gather.6 = f32[64,64,16]{1,2,0:T(8,128)S(1)} all-gather(f32[1,64,16]{1,2,0:T(8,128)S(1)} %fusion.22), channel_id=1, replica_groups=mesh['sep'=8,'row'=8,'col'=8] {'row','col'}, dimensions={0}, use_global_device_ids=true | all-gather | bytes 266240 | tf_op jit(solution)/shard_map/while/body/eval_jaxpr/all_gather | solution.py:52
  1773.3 49.5 %all-gather.7 = f32[64,64,16]{1,2,0:T(8,128)S(1)} all-gather(f32[1,64,16]{1,2,0:T(8,128)S(1)} %bitcast.71), channel_id=1, replica_groups=mesh['sep'=8,'row'=8,'col'=8] {'row','col'}, dimensions={0}, use_global_device_ids=true | all-gather | bytes 266240 | tf_op jit(solution)/shard_map/while/body/eval_jaxpr/all_gather | solution.py:53
  1827.4 9.7 collective-permute-done
  (314 shorter events, 122.2 us)
Async XLA Ops:
  58.1 1.2 copy-start
  109.9 1.0 copy-start.1
  112.5 11.7 collective-permute-start
  172.3 1.2 copy-start
  224.1 1.0 copy-start.1
  226.7 11.7 collective-permute-start
  286.5 1.2 copy-start
  338.3 1.0 copy-start.1
  340.9 11.7 collective-permute-start
  400.7 1.2 copy-start
  452.5 1.0 copy-start.1
  455.1 11.7 collective-permute-start
  514.9 1.2 copy-start
  566.7 1.0 copy-start.1
  569.3 11.7 collective-permute-start
  629.1 1.2 copy-start
  681.0 1.0 copy-start.1
  683.5 11.7 collective-permute-start
  743.3 1.2 copy-start
  795.2 1.0 copy-start.1
  797.7 11.7 collective-permute-start
  857.5 1.2 copy-start
  909.4 1.0 copy-start.1
  911.9 11.7 collective-permute-start
  971.7 1.2 copy-start
  1023.6 1.0 copy-start.1
  1026.1 11.7 collective-permute-start
  1085.9 1.2 copy-start
  1137.8 1.0 copy-start.1
  1140.3 11.7 collective-permute-start
  1200.1 1.2 copy-start
  1252.0 1.0 copy-start.1
  1254.5 11.7 collective-permute-start
  1314.3 1.2 copy-start
  1366.2 1.0 copy-start.1
  1368.7 11.7 collective-permute-start
  1428.5 1.2 copy-start
  1480.4 1.0 copy-start.1
  1482.9 11.7 collective-permute-start
  1542.7 1.2 copy-start
  1594.6 1.0 copy-start.1
  1597.1 11.7 collective-permute-start
  1657.0 1.2 copy-start
  1708.8 1.0 copy-start.1
  1711.3 11.7 collective-permute-start
  1771.2 1.2 copy-start
  1823.0 1.0 copy-start.1
  1825.5 11.7 collective-permute-start
  (3 other events, 2.0 us)
where the time goes:
time: 1840 us
  blocking collectives  1570 us (85%)
  waiting for transfers between devices  155 us (8%)
  local copies, waits for them, and re-layouts  33.2 us (2%)
  starting transfers between devices  31.4 us (2%)
  other arithmetic  25.5 us (1%)
  matrix products  23 us (1%)
    all_gather x16, blocking collectives, one_turn(): lax.all_gather(solved, ('row', 'col'), axis=1, tiled=True)  792 us
    all_gather x16, blocking collectives, one_turn(): lax.all_gather(resid, ('row', 'col'), axis=1, tiled=True)  776 us
    ppermute x16, waiting for transfers between devices, passed_along(): return lax.ppermute(block, axis, route)  155 us
  transfers between devices with their start and end apart: 16, of which 16 were waited for; matrix products, arithmetic and copies ran while one was open for 0% of the time, Pallas kernels for 0%

commit v1 on v0

--- a/solution.py
+++ b/solution.py
@@ -49,7 +49,14 @@
         batch_now = jnp.clip(batch_now, 0, batches - 1)
         given = lax.dynamic_index_in_dim(right_sides, batch_now, 0, keepdims=False)
         resid = given - lax.dynamic_slice_in_dim(carried, own_level * own_rows, own_rows, 1)
-        solved = solve_piece(lax.all_gather(resid, ("row", "col"), axis=1, tiled=True))
+        solved = solve_piece(
+            jnp.concatenate(
+                lax.all_to_all(
+                    jnp.stack([resid] * lax.axis_size(("row", "col"))), ("row", "col"), 0, 0
+                ),
+                axis=1,
+            )
+        )
         update = lower_piece(lax.all_gather(solved, ("row", "col"), axis=1, tiled=True))
         update = jnp.where(live[None, :], update, jnp.float32(0.0))
         carried = carried.at[:, places].add(update)

time: 1840 us -> 1410 us (0.77)
  blocking collectives: 1570 us -> 783 us
  waiting for transfers between devices: 155 us -> 350 us
  starting transfers between devices: 31.4 us -> 137 us
  local copies, waits for them, and re-layouts: 33.2 us -> 72.1 us
    all_gather x16 -> x0, blocking collectives: 776 us -> none  [one_turn(): lax.all_gather(resid, ('row', 'col'), axis=1, tiled=True)]
    all_to_all x0 -> x16, waiting for transfers between devices: none -> 195 us  [one_turn(): lax.all_to_all(jnp.stack([resid] * lax.axis_size(('row', 'col'))), ('row'...]
    all_to_all x0 -> x16, starting transfers between devices: none -> 105 us  [one_turn(): lax.all_to_all(jnp.stack([resid] * lax.axis_size(('row', 'col'))), ('row'...]
    while x128, local copies, waits for them, and re-layouts: 24.4 us -> 49.1 us
    all_to_all x0 -> x16, other arithmetic: none -> 18.7 us  [one_turn(): lax.all_to_all(jnp.stack([resid] * lax.axis_size(('row', 'col'))), ('row'...]
  transfers between devices with their start and end apart: 16 -> 32, of which waited for: 16 -> 32; matrix products, arithmetic and copies ran while one was open for 0% -> 1% of each run, Pallas kernels for 0% -> 0%
where the time goes in v1:
time: 1410 us
  blocking collectives  783 us (56%)
  waiting for transfers between devices  350 us (25%)
  starting transfers between devices  137 us (10%)
  local copies, waits for them, and re-layouts  72.1 us (5%)
  other arithmetic  43.2 us (3%)
  matrix products  23 us (2%)
    all_gather x16, blocking collectives, one_turn(): lax.all_gather(solved, ('row', 'col'), axis=1, tiled=True)  783 us
    all_to_all x16, waiting for transfers between devices, one_turn(): lax.all_to_all(jnp.stack([resid] * lax.axis_size(('row', 'col'))), ('row'...  195 us
    ppermute x16, waiting for transfers between devices, passed_along(): return lax.ppermute(block, axis, route)  155 us
    all_to_all x16, starting transfers between devices, one_turn(): lax.all_to_all(jnp.stack([resid] * lax.axis_size(('row', 'col'))), ('row'...  105 us
    while x128, local copies, waits for them, and re-layouts  49.1 us
    ppermute x16, starting transfers between devices, passed_along(): return lax.ppermute(block, axis, route)  31.4 us
  transfers between devices with their start and end apart: 32, of which 32 were waited for; matrix products, arithmetic and copies ran while one was open for 1% of the time, Pallas kernels for 0%

profile of v1, /device:TPU:32, one launch (start us, length us, event | category | flops | bytes accessed | tf_op | source)
XLA Modules:
  0.0 1410.6 jit_solution(3811199146350053031)
XLA Ops:
  1.4 1408.6 %while.18 = (s32[]{:T(128)}, f32[16,512]{0,1:T(8,128)S(1)}, f32[2,16,64]{2,1,0:T(8,128)S(1)}, s32[32]{0:T(128)S(1)}, f32[2,16,64]{2,1,0:T(8,128)S(1)}, /*index=5...) while((s32[]{:T(128)}, f32[16,512]{0,1:T(8,128)S(1)}, ...), condition=%wide.region_2.3_spmd.clone, body=%wide.region_0.2_spmd.clone.sunk | while | flops 75500688 | bytes 13656974 | solution.py:73
  2.7 13.8 all-to-all-start
  17.1 12.2 all-to-all-done
  33.3 48.9 %all-gather.3 = f32[64,64,16]{1,2,0:T(8,128)S(1)} all-gather(f32[1,64,16]{1,2,0:T(8,128)S(1)} %bitcast.65), channel_id=1, replica_groups=mesh['sep'=8,'row'=8,'col'=8] {'row','col'}, dimensions={0}, use_global_device_ids=true | all-gather | bytes 266240 | tf_op jit(solution)/shard_map/while/body/eval_jaxpr/all_gather | solution.py:60
  104.7 12.2 all-to-all-done
  120.9 48.9 %all-gather.3 = f32[64,64,16]{1,2,0:T(8,128)S(1)} all-gather(f32[1,64,16]{1,2,0:T(8,128)S(1)} %bitcast.65), channel_id=1, replica_groups=mesh['sep'=8,'row'=8,'col'=8] {'row','col'}, dimensions={0}, use_global_device_ids=true | all-gather | bytes 266240 | tf_op jit(solution)/shard_map/while/body/eval_jaxpr/all_gather | solution.py:60
  174.4 9.7 collective-permute-done
  192.2 12.2 all-to-all-done
  208.4 48.9 %all-gather.3 = f32[64,64,16]{1,2,0:T(8,128)S(1)} all-gather(f32[1,64,16]{1,2,0:T(8,128)S(1)} %bitcast.65), channel_id=1, replica_groups=mesh['sep'=8,'row'=8,'col'=8] {'row','col'}, dimensions={0}, use_global_device_ids=true | all-gather | bytes 266240 | tf_op jit(solution)/shard_map/while/body/eval_jaxpr/all_gather | solution.py:60
  262.0 9.7 collective-permute-done
  279.8 12.2 all-to-all-done
  296.0 48.9 %all-gather.3 = f32[64,64,16]{1,2,0:T(8,128)S(1)} all-gather(f32[1,64,16]{1,2,0:T(8,128)S(1)} %bitcast.65), channel_id=1, replica_groups=mesh['sep'=8,'row'=8,'col'=8] {'row','col'}, dimensions={0}, use_global_device_ids=true | all-gather | bytes 266240 | tf_op jit(solution)/shard_map/while/body/eval_jaxpr/all_gather | solution.py:60
  349.5 9.7 collective-permute-done
  367.4 12.2 all-to-all-done
  383.5 48.9 %all-gather.3 = f32[64,64,16]{1,2,0:T(8,128)S(1)} all-gather(f32[1,64,16]{1,2,0:T(8,128)S(1)} %bitcast.65), channel_id=1, replica_groups=mesh['sep'=8,'row'=8,'col'=8] {'row','col'}, dimensions={0}, use_global_device_ids=true | all-gather | bytes 266240 | tf_op jit(solution)/shard_map/while/body/eval_jaxpr/all_gather | solution.py:60
  437.1 9.7 collective-permute-done
  454.9 12.2 all-to-all-done
  471.1 48.9 %all-gather.3 = f32[64,64,16]{1,2,0:T(8,128)S(1)} all-gather(f32[1,64,16]{1,2,0:T(8,128)S(1)} %bitcast.65), channel_id=1, replica_groups=mesh['sep'=8,'row'=8,'col'=8] {'row','col'}, dimensions={0}, use_global_device_ids=true | all-gather | bytes 266240 | tf_op jit(solution)/shard_map/while/body/eval_jaxpr/all_gather | solution.py:60
  524.7 9.7 collective-permute-done
  542.5 12.2 all-to-all-done
  558.7 48.9 %all-gather.3 = f32[64,64,16]{1,2,0:T(8,128)S(1)} all-gather(f32[1,64,16]{1,2,0:T(8,128)S(1)} %bitcast.65), channel_id=1, replica_groups=mesh['sep'=8,'row'=8,'col'=8] {'row','col'}, dimensions={0}, use_global_device_ids=true | all-gather | bytes 266240 | tf_op jit(solution)/shard_map/while/body/eval_jaxpr/all_gather | solution.py:60
  612.2 9.7 collective-permute-done
  630.0 12.2 all-to-all-done
  646.2 48.9 %all-gather.3 = f32[64,64,16]{1,2,0:T(8,128)S(1)} all-gather(f32[1,64,16]{1,2,0:T(8,128)S(1)} %bitcast.65), channel_id=1, replica_groups=mesh['sep'=8,'row'=8,'col'=8] {'row','col'}, dimensions={0}, use_global_device_ids=true | all-gather | bytes 266240 | tf_op jit(solution)/shard_map/while/body/eval_jaxpr/all_gather | solution.py:60
  699.8 9.7 collective-permute-done
  717.6 12.2 all-to-all-done
  733.8 48.9 %all-gather.3 = f32[64,64,16]{1,2,0:T(8,128)S(1)} all-gather(f32[1,64,16]{1,2,0:T(8,128)S(1)} %bitcast.65), channel_id=1, replica_groups=mesh['sep'=8,'row'=8,'col'=8] {'row','col'}, dimensions={0}, use_global_device_ids=true | all-gather | bytes 266240 | tf_op jit(solution)/shard_map/while/body/eval_jaxpr/all_gather | solution.py:60
  787.3 9.7 collective-permute-done
  805.2 12.2 all-to-all-done
  821.3 48.9 %all-gather.3 = f32[64,64,16]{1,2,0:T(8,128)S(1)} all-gather(f32[1,64,16]{1,2,0:T(8,128)S(1)} %bitcast.65), channel_id=1, replica_groups=mesh['sep'=8,'row'=8,'col'=8] {'row','col'}, dimensions={0}, use_global_device_ids=true | all-gather | bytes 266240 | tf_op jit(solution)/shard_map/while/body/eval_jaxpr/all_gather | solution.py:60
  874.9 9.7 collective-permute-done
  892.7 12.2 all-to-all-done
  908.9 48.9 %all-gather.3 = f32[64,64,16]{1,2,0:T(8,128)S(1)} all-gather(f32[1,64,16]{1,2,0:T(8,128)S(1)} %bitcast.65), channel_id=1, replica_groups=mesh['sep'=8,'row'=8,'col'=8] {'row','col'}, dimensions={0}, use_global_device_ids=true | all-gather | bytes 266240 | tf_op jit(solution)/shard_map/while/body/eval_jaxpr/all_gather | solution.py:60
  962.4 9.7 collective-permute-done
  980.3 12.2 all-to-all-done
  996.5 48.9 %all-gather.3 = f32[64,64,16]{1,2,0:T(8,128)S(1)} all-gather(f32[1,64,16]{1,2,0:T(8,128)S(1)} %bitcast.65), channel_id=1, replica_groups=mesh['sep'=8,'row'=8,'col'=8] {'row','col'}, dimensions={0}, use_global_device_ids=true | all-gather | bytes 266240 | tf_op jit(solution)/shard_map/while/body/eval_jaxpr/all_gather | solution.py:60
  1050.0 9.7 collective-permute-done
  1067.8 12.2 all-to-all-done
  1084.0 48.9 %all-gather.3 = f32[64,64,16]{1,2,0:T(8,128)S(1)} all-gather(f32[1,64,16]{1,2,0:T(8,128)S(1)} %bitcast.65), channel_id=1, replica_groups=mesh['sep'=8,'row'=8,'col'=8] {'row','col'}, dimensions={0}, use_global_device_ids=true | all-gather | bytes 266240 | tf_op jit(solution)/shard_map/while/body/eval_jaxpr/all_gather | solution.py:60
  1137.6 9.7 collective-permute-done
  1155.4 12.2 all-to-all-done
  1171.6 48.9 %all-gather.3 = f32[64,64,16]{1,2,0:T(8,128)S(1)} all-gather(f32[1,64,16]{1,2,0:T(8,128)S(1)} %bitcast.65), channel_id=1, replica_groups=mesh['sep'=8,'row'=8,'col'=8] {'row','col'}, dimensions={0}, use_global_device_ids=true | all-gather | bytes 266240 | tf_op jit(solution)/shard_map/while/body/eval_jaxpr/all_gather | solution.py:60
  1225.1 9.7 collective-permute-done
  1243.0 12.2 all-to-all-done
  1259.1 48.9 %all-gather.3 = f32[64,64,16]{1,2,0:T(8,128)S(1)} all-gather(f32[1,64,16]{1,2,0:T(8,128)S(1)} %bitcast.65), channel_id=1, replica_groups=mesh['sep'=8,'row'=8,'col'=8] {'row','col'}, dimensions={0}, use_global_device_ids=true | all-gather | bytes 266240 | tf_op jit(solution)/shard_map/while/body/eval_jaxpr/all_gather | solution.py:60
  1312.7 9.7 collective-permute-done
  1330.5 12.2 all-to-all-done
  1346.7 48.9 %all-gather.3 = f32[64,64,16]{1,2,0:T(8,128)S(1)} all-gather(f32[1,64,16]{1,2,0:T(8,128)S(1)} %bitcast.65), channel_id=1, replica_groups=mesh['sep'=8,'row'=8,'col'=8] {'row','col'}, dimensions={0}, use_global_device_ids=true | all-gather | bytes 266240 | tf_op jit(solution)/shard_map/while/body/eval_jaxpr/all_gather | solution.py:60
  (426 shorter events, 280.0 us)
Async XLA Ops:
  2.7 26.7 %all-to-all-start = ((f32[64,1,1024]{2,1,0:T(1,128)}), f32[64,1,1024]{2,1,0:T(1,128)S(1)}, u32[]{:S(2)}, u32[]{:S(2)}) async-start(f32[64,1,1024]{2,1,0:T(1,128)} %reshape.71), calls=%async_computation | async-start | bytes 524288 | tf_op jit(solution)/shard_map/while/body/eval_jaxpr/all_to_all | solution.py:54
  31.2 1.2 copy-start
  84.9 11.7 collective-permute-start
  97.9 19.0 %all-to-all-start = ((f32[64,1,1024]{2,1,0:T(1,128)}), f32[64,1,1024]{2,1,0:T(1,128)S(1)}, u32[]{:S(2)}, u32[]{:S(2)}) async-start(f32[64,1,1024]{2,1,0:T(1,128)} %reshape.71), calls=%async_computation | async-start | bytes 524288 | tf_op jit(solution)/shard_map/while/body/eval_jaxpr/all_to_all | solution.py:54
  118.7 1.2 copy-start
  172.5 11.7 collective-permute-start
  185.5 19.0 %all-to-all-start = ((f32[64,1,1024]{2,1,0:T(1,128)}), f32[64,1,1024]{2,1,0:T(1,128)S(1)}, u32[]{:S(2)}, u32[]{:S(2)}) async-start(f32[64,1,1024]{2,1,0:T(1,128)} %reshape.71), calls=%async_computation | async-start | bytes 524288 | tf_op jit(solution)/shard_map/while/body/eval_jaxpr/all_to_all | solution.py:54
  206.3 1.2 copy-start
  260.0 11.7 collective-permute-start
  273.0 19.0 %all-to-all-start = ((f32[64,1,1024]{2,1,0:T(1,128)}), f32[64,1,1024]{2,1,0:T(1,128)S(1)}, u32[]{:S(2)}, u32[]{:S(2)}) async-start(f32[64,1,1024]{2,1,0:T(1,128)} %reshape.71), calls=%async_computation | async-start | bytes 524288 | tf_op jit(solution)/shard_map/while/body/eval_jaxpr/all_to_all | solution.py:54
  293.8 1.2 copy-start
  347.6 11.7 collective-permute-start
  360.6 19.0 %all-to-all-start = ((f32[64,1,1024]{2,1,0:T(1,128)}), f32[64,1,1024]{2,1,0:T(1,128)S(1)}, u32[]{:S(2)}, u32[]{:S(2)}) async-start(f32[64,1,1024]{2,1,0:T(1,128)} %reshape.71), calls=%async_computation | async-start | bytes 524288 | tf_op jit(solution)/shard_map/while/body/eval_jaxpr/all_to_all | solution.py:54
  381.4 1.2 copy-start
  435.2 11.7 collective-permute-start
  448.1 19.0 %all-to-all-start = ((f32[64,1,1024]{2,1,0:T(1,128)}), f32[64,1,1024]{2,1,0:T(1,128)S(1)}, u32[]{:S(2)}, u32[]{:S(2)}) async-start(f32[64,1,1024]{2,1,0:T(1,128)} %reshape.71), calls=%async_computation | async-start | bytes 524288 | tf_op jit(solution)/shard_map/while/body/eval_jaxpr/all_to_all | solution.py:54
  469.0 1.2 copy-start
  522.7 11.7 collective-permute-start
  535.7 19.0 %all-to-all-start = ((f32[64,1,1024]{2,1,0:T(1,128)}), f32[64,1,1024]{2,1,0:T(1,128)S(1)}, u32[]{:S(2)}, u32[]{:S(2)}) async-start(f32[64,1,1024]{2,1,0:T(1,128)} %reshape.71), calls=%async_computation | async-start | bytes 524288 | tf_op jit(solution)/shard_map/while/body/eval_jaxpr/all_to_all | solution.py:54
  556.5 1.2 copy-start
  610.3 11.7 collective-permute-start
  623.3 19.0 %all-to-all-start = ((f32[64,1,1024]{2,1,0:T(1,128)}), f32[64,1,1024]{2,1,0:T(1,128)S(1)}, u32[]{:S(2)}, u32[]{:S(2)}) async-start(f32[64,1,1024]{2,1,0:T(1,128)} %reshape.71), calls=%async_computation | async-start | bytes 524288 | tf_op jit(solution)/shard_map/while/body/eval_jaxpr/all_to_all | solution.py:54
  644.1 1.2 copy-start
  697.8 11.7 collective-permute-start
  710.8 19.0 %all-to-all-start = ((f32[64,1,1024]{2,1,0:T(1,128)}), f32[64,1,1024]{2,1,0:T(1,128)S(1)}, u32[]{:S(2)}, u32[]{:S(2)}) async-start(f32[64,1,1024]{2,1,0:T(1,128)} %reshape.71), calls=%async_computation | async-start | bytes 524288 | tf_op jit(solution)/shard_map/while/body/eval_jaxpr/all_to_all | solution.py:54
  731.6 1.2 copy-start
  785.4 11.7 collective-permute-start
  798.4 19.0 %all-to-all-start = ((f32[64,1,1024]{2,1,0:T(1,128)}), f32[64,1,1024]{2,1,0:T(1,128)S(1)}, u32[]{:S(2)}, u32[]{:S(2)}) async-start(f32[64,1,1024]{2,1,0:T(1,128)} %reshape.71), calls=%async_computation | async-start | bytes 524288 | tf_op jit(solution)/shard_map/while/body/eval_jaxpr/all_to_all | solution.py:54
  819.2 1.2 copy-start
  873.0 11.7 collective-permute-start
  885.9 19.0 %all-to-all-start = ((f32[64,1,1024]{2,1,0:T(1,128)}), f32[64,1,1024]{2,1,0:T(1,128)S(1)}, u32[]{:S(2)}, u32[]{:S(2)}) async-start(f32[64,1,1024]{2,1,0:T(1,128)} %reshape.71), calls=%async_computation | async-start | bytes 524288 | tf_op jit(solution)/shard_map/while/body/eval_jaxpr/all_to_all | solution.py:54
  906.7 1.2 copy-start
  960.5 11.7 collective-permute-start
  973.5 19.0 %all-to-all-start = ((f32[64,1,1024]{2,1,0:T(1,128)}), f32[64,1,1024]{2,1,0:T(1,128)S(1)}, u32[]{:S(2)}, u32[]{:S(2)}) async-start(f32[64,1,1024]{2,1,0:T(1,128)} %reshape.71), calls=%async_computation | async-start | bytes 524288 | tf_op jit(solution)/shard_map/while/body/eval_jaxpr/all_to_all | solution.py:54
  994.3 1.2 copy-start
  1048.1 11.7 collective-permute-start
  1061.0 19.0 %all-to-all-start = ((f32[64,1,1024]{2,1,0:T(1,128)}), f32[64,1,1024]{2,1,0:T(1,128)S(1)}, u32[]{:S(2)}, u32[]{:S(2)}) async-start(f32[64,1,1024]{2,1,0:T(1,128)} %reshape.71), calls=%async_computation | async-start | bytes 524288 | tf_op jit(solution)/shard_map/while/body/eval_jaxpr/all_to_all | solution.py:54
  1081.9 1.2 copy-start
  1135.6 11.7 collective-permute-start
  1148.6 19.0 %all-to-all-start = ((f32[64,1,1024]{2,1,0:T(1,128)}), f32[64,1,1024]{2,1,0:T(1,128)S(1)}, u32[]{:S(2)}, u32[]{:S(2)}) async-start(f32[64,1,1024]{2,1,0:T(1,128)} %reshape.71), calls=%async_computation | async-start | bytes 524288 | tf_op jit(solution)/shard_map/while/body/eval_jaxpr/all_to_all | solution.py:54
  1169.4 1.2 copy-start
  1223.2 11.7 collective-permute-start
  1236.2 19.0 %all-to-all-start = ((f32[64,1,1024]{2,1,0:T(1,128)}), f32[64,1,1024]{2,1,0:T(1,128)S(1)}, u32[]{:S(2)}, u32[]{:S(2)}) async-start(f32[64,1,1024]{2,1,0:T(1,128)} %reshape.71), calls=%async_computation | async-start | bytes 524288 | tf_op jit(solution)/shard_map/while/body/eval_jaxpr/all_to_all | solution.py:54
  1257.0 1.2 copy-start
  1310.8 11.7 collective-permute-start
  1323.7 19.0 %all-to-all-start = ((f32[64,1,1024]{2,1,0:T(1,128)}), f32[64,1,1024]{2,1,0:T(1,128)S(1)}, u32[]{:S(2)}, u32[]{:S(2)}) async-start(f32[64,1,1024]{2,1,0:T(1,128)} %reshape.71), calls=%async_computation | async-start | bytes 524288 | tf_op jit(solution)/shard_map/while/body/eval_jaxpr/all_to_all | solution.py:54
  1344.5 1.2 copy-start
  1398.3 11.7 collective-permute-start
  (19 other events, 18.7 us)
